TPU v7x, 256 devices: a whole 4x4x8 slice. The times are simulated.
256 devices in a mesh: tm: 64 (over x, z_lo, y), feed: 4 (over z_hi, core).
Axes of the slice: x: 4, y: 4, z: 8 (z_hi: 2, z_lo: 4; z = z_hi * 4 + z_lo), core: 2. Of those that a mesh axis runs over, the one named last changes fastest.
Arguments:
- voltages: bfloat16 [1024, 131072], P('feed', 'tm'), may hold values from -6 to 6
- coefficients: float32 [16, 2048], replicated, may hold values from -1.5 to 1.5
- beam_weights: bfloat16 [1024, 1024, 2, 512], P('tm', 'feed'), may hold values from -0.1875 to 0.1875
Outputs:
- beam_power: float32 [8, 1024, 512], P(None, 'tm', 'feed')
All inputs are finite; a program needn't handle non-finite values.
Results may differ from a plain program's by a relative error of at most 0.0025.
Values may be sent and summed in bfloat16 or wider, within the bound.
No kernel may reach another device: no remote copies, remote signals or barrier semaphores. Data moves between devices by JAX's collectives and lax.ppermute only.
A program may use at most 128 MiB of HBM per device.

v0:
```python
import math
import jax
import jax.numpy as jnp
from jax import lax
from jax.sharding import PartitionSpec as P

INTEG = 8


def shifted(value, axis, steps):
    count = lax.axis_size(axis)
    initial, last = (max(0, -steps), min(count, count - steps))
    return lax.ppermute(value, axis, [(source, source + steps) for source in range(initial, last)])


def dft_table(frame_len):
    channels = frame_len // 2
    sample = lax.broadcasted_iota(jnp.int32, (frame_len, channels), 0)
    channel = lax.broadcasted_iota(jnp.int32, (frame_len, channels), 1)
    angles = 2.0 * math.pi / frame_len * (sample * channel % frame_len).astype(jnp.float32)
    norming = 1.0 / math.sqrt(frame_len)
    stacked = jnp.stack([jnp.cos(angles) * norming, -jnp.sin(angles) * norming], axis=2)
    return stacked.reshape(frame_len, 2 * channels).astype(jnp.bfloat16)


def polyphase(extended, coefficients, frames):
    tap_count = coefficients.shape[0]
    running = jnp.zeros((extended.shape[0], frames, extended.shape[2]), jnp.float32)
    for tap_index in range(tap_count):
        running = running + coefficients[tap_index][None, None, :] * extended[
            :, tap_index : tap_index + frames, :
        ].astype(jnp.float32)
    return running.astype(jnp.bfloat16)


def sign_pairs(arranged):
    real_part = arranged[:, :, 0]
    imag_part = arranged[:, :, 1]
    for_real = jnp.stack([real_part, -imag_part], axis=2)
    for_imag = jnp.stack([imag_part, real_part], axis=2)
    return (for_real, for_imag)


def form_beams(for_real, for_imag, weight_part):
    beam_re = jnp.einsum(
        "tcrf,cfrb->bct", for_real, weight_part, preferred_element_type=jnp.float32
    )
    beam_im = jnp.einsum(
        "tcrf,cfrb->bct", for_imag, weight_part, preferred_element_type=jnp.float32
    )
    return jnp.stack([beam_re, beam_im], axis=1)


def detect(beams):
    energy = jnp.sum(beams * beams, axis=1)
    beam_count, per_group, total_frames = energy.shape
    binned = jnp.mean(energy.reshape(beam_count, per_group, total_frames // INTEG, INTEG), axis=3)
    return jnp.transpose(binned, (2, 1, 0))


def local(voltages, coefficients, beam_weights):
    feeds_here, samples = voltages.shape
    tap_count, frame_len = coefficients.shape
    look_ahead = tap_count - 1
    transform = dft_table(frame_len)
    frames = samples // frame_len
    blocks = voltages.reshape(feeds_here, frames, frame_len)
    neighbours = min((look_ahead + frames - 1) // frames, lax.axis_size("tm") - 1)
    pieces = [blocks]
    for distance in range(1, neighbours + 1):
        pieces.append(shifted(blocks, "tm", -distance))
    extended = jnp.concatenate(pieces, axis=1)
    filtered = polyphase(extended, coefficients, frames)
    spectra = jnp.einsum(
        "ftk,kc->tcf", filtered, transform, preferred_element_type=jnp.float32
    ).astype(jnp.bfloat16)
    turned = lax.all_to_all(spectra, "tm", split_axis=1, concat_axis=0, tiled=True)
    total_frames, paired, feed_width = turned.shape
    per_group = paired // 2
    arranged = turned.reshape(total_frames, per_group, 2, feed_width)
    for_real, for_imag = sign_pairs(arranged)
    beams = lax.psum_scatter(
        form_beams(for_real, for_imag, beam_weights), "feed", scatter_dimension=0, tiled=True
    )
    return detect(beams)


def solution(mesh):
    placed = (P("feed", "tm"), P(), P("tm", "feed", None, None))
    return jax.shard_map(
        local, mesh=mesh, in_specs=placed, out_specs=P(None, "tm", "feed"), check_vma=False
    )
```

profile of v0, /device:TPU:1, one launch (start us, length us, event | category | flops | bytes accessed | tf_op | source)
XLA Modules:
  0.0 792.3 jit_solution(8852012217520192033)
XLA Ops:
  6.5 1.3 collective-permute-start.14
  7.8 1.3 collective-permute-start.13
  9.1 1.3 collective-permute-start.12
  10.4 1.3 collective-permute-start.11
  11.7 1.3 collective-permute-start.10
  13.0 46.5 %collective-permute-done.14 = bf16[256,1,2048]{2,0,1:T(8,128)(2,1)S(1)} collective-permute-done((bf16[256,1,2048]{2,0,1:T(8,128)(2,1)}, bf16[256,1,2048]{2,0,1:T(8,128)(2,1)S(1)}, u32[]{:S(2)}, u32[]{:S(2)}) %collective-permute-start.14) | collective-permute-done | bytes 1048608 | tf_op jit(solution)/shard_map/ppermute | solution.py:13
  59.5 1.3 collective-permute-start.9
  60.8 1.3 collective-permute-start.8
  62.1 1.3 collective-permute-start.7
  63.4 1.3 collective-permute-start.6
  64.7 129.1 %collective-permute-done.10 = bf16[256,1,2048]{2,0,1:T(8,128)(2,1)S(1)} collective-permute-done((bf16[256,1,2048]{2,0,1:T(8,128)(2,1)}, bf16[256,1,2048]{2,0,1:T(8,128)(2,1)S(1)}, u32[]{:S(2)}, u32[]{:S(2)}) %collective-permute-start.10) | collective-permute-done | bytes 1048608 | tf_op jit(solution)/shard_map/ppermute | solution.py:13
  193.8 1.3 collective-permute-start.5
  195.1 17.9 %collective-permute-done.9 = bf16[256,1,2048]{2,0,1:T(8,128)(2,1)S(1)} collective-permute-done((bf16[256,1,2048]{2,0,1:T(8,128)(2,1)}, bf16[256,1,2048]{2,0,1:T(8,128)(2,1)S(1)}, u32[]{:S(2)}, u32[]{:S(2)}) %collective-permute-start.9) | collective-permute-done | bytes 1048608 | tf_op jit(solution)/shard_map/ppermute | solution.py:13
  213.0 1.3 collective-permute-start.4
  214.2 33.5 %collective-permute-done.8 = bf16[256,1,2048]{2,0,1:T(8,128)(2,1)S(1)} collective-permute-done((bf16[256,1,2048]{2,0,1:T(8,128)(2,1)}, bf16[256,1,2048]{2,0,1:T(8,128)(2,1)S(1)}, u32[]{:S(2)}, u32[]{:S(2)}) %collective-permute-start.8) | collective-permute-done | bytes 1048608 | tf_op jit(solution)/shard_map/ppermute | solution.py:13
  247.8 1.3 collective-permute-start.3
  249.1 1.3 collective-permute-start.2
  250.4 1.3 collective-permute-start.1
  251.8 1.0 copy-done.9
  252.8 1.3 collective-permute-start
  254.1 34.9 %multiply_convert_fusion = (bf16[2048,1024,1]{1,0,2:T(8,128)(2,1)S(1)}, bf16[2048,1024,1]{1,0,2:T(8,128)(2,1)}) fusion(), kind=kLoop, calls=%fused_computation.7 | loop fusion | flops 39845888 | bytes 8388608 | tf_op jit(solution)/shard_map/convert.1
  289.0 6.2 pad_maximum_fusion
  295.2 21.5 %copy.22 = bf16[2048,1024,2]{0,2,1:T(2,128)(2,1)} copy(bf16[2048,1024,2]{1,0,2:T(8,128)(2,1)} %pad_maximum_fusion) | data formatting | bytes 16777216 | tf_op jit(solution)/shard_map/stack | solution.py:22
  316.7 13.2 %convert_element_type.85 = bf16[2048,2048]{0,1:T(8,128)(2,1)} reshape(bf16[2048,1024,2]{0,2,1:T(2,128)(2,1)} %copy.22) | data formatting | bytes 16777216 | tf_op jit(solution)/shard_map/convert_element_type | solution.py:23
  329.9 0.1 fusion.59
  330.0 45.3 %collective-permute-done.2 = bf16[256,1,2048]{2,0,1:T(8,128)(2,1)} collective-permute-done((bf16[256,1,2048]{2,0,1:T(8,128)(2,1)}, bf16[256,1,2048]{2,0,1:T(8,128)(2,1)}, u32[]{:S(2)}, u32[]{:S(2)}) %collective-permute-start.2) | collective-permute-done | bytes 1048608 | tf_op jit(solution)/shard_map/ppermute | solution.py:13
  375.3 14.0 %fusion.10 = bf16[1,2048,256]{2,1,0:T(8,128)(2,1)S(1)} fusion(bf16[2048,2048]{0,1:T(8,128)(2,1)} %convert_element_type.85, bf16[256,1,2048]{2,0,1:T(8,128)(2,1)S(1)} %collective-permute-done.14, bf16[256,1,2048]{2,0,1:T(8,128)(2,1)S(1)} %collective-permute-done.13, bf16[256,1,2048]{2,0,1:T(8,128)(2,1)} %copy-done.2, bf16[256,1,2048]{2,0,1:T(8,128)(2,1)} %copy-done.3, ...), kind=kOutput, calls=%fused_computation.18 | convolution fusion | flops 2173173760 | bytes 26345472 | tf_op jit(solution)/shard_map/ftk,kc->tcf/dot_general | solution.py:74
  389.3 11.7 %copy.44 = bf16[1,2048,256]{2,0,1:T(2,128)(2,1)S(1)} copy(bf16[1,2048,256]{2,1,0:T(8,128)(2,1)S(1)} %fusion.10) | data formatting | bytes 2097152 | tf_op jit(solution)/shard_map/convert_element_type | solution.py:76
  401.1 0.5 broadcast.118
  401.6 10.8 %reduce.2 = bf16[2048,256]{1,0:T(8,128)(2,1)S(1)} reduce(bf16[2048,1,256]{2,1,0:T(2,128)(2,1)S(1)} %bitcast.83, bf16[]{:T(256)} %broadcast.118), dimensions={1}, to_apply=%bitcast.82.reduce_sub_computation | reduce | bytes 2097154
  412.4 0.3 reshape.151
  412.6 198.2 %all_to_all.4 = bf16[64,2,4096]{2,1,0:T(2,128)(2,1)S(1)} all-to-all(bf16[64,2,4096]{2,1,0:T(2,128)(2,1)S(1)} %reshape.151), channel_id=1, replica_groups=mesh['tm'=64,'feed'=4] {'tm'}, dimensions={0} | all-to-all | bytes 2097152 | tf_op jit(solution)/shard_map/all_to_all | solution.py:77
  610.8 1.0 reshape.152
  611.9 11.0 %bitcast_reduce_fusion.1 = bf16[2048,256]{1,0:T(8,128)(2,1)S(1)} fusion(bf16[2048,1,256]{2,1,0:T(2,128)(2,1)S(1)} %reshape.152), kind=kLoop, calls=%fused_computation.67 | loop fusion | bytes 2097152 | tf_op jit(solution)/shard_map/all_to_all | solution.py:77
  622.9 0.4 reshape.146
  623.3 2.4 fusion.58
  625.7 0.6 copy.32
  626.2 0.0 slice-start
  626.3 0.6 fusion.57
  626.9 0.0 slice-start.1
  626.9 5.5 fusion.29
  632.4 2.0 fusion.26
  634.4 2.5 pad_maximum_fusion.1
  636.9 0.0 reduce-scatter.2.cloned.1.call-update
  636.9 146.3 %reduce-scatter.2.cloned.1.call-done = f32[128,2,16,64]{0,3,2,1:T(8,128)} async-done(((f32[512,2,16,64]{0,3,2,1:T(8,128)}), f32[128,2,16,64]{0,3,2,1:T(8,128)}) %reduce-scatter.2.cloned.1.call-update) | async-done | bytes 1048592 | tf_op jit(solution)/shard_map/reduce_scatter | solution.py:82
  783.2 1.4 multiply_reduce_fusion
  784.6 0.1 bitcast_reduce_fusion
  784.8 0.6 copy.28
  (34 shorter events, 0.1 us)
Async XLA Ops:
  6.5 776.7 %reduce-scatter.2.cloned.1.call-start = ((), (), s32[]{:S(2)}) async-start(), calls=%async_computation.2 | async-start | bytes 5242880 | tf_op jit(solution)/shard_map/reduce_scatter | solution.py:82
  6.5 52.9 %collective-permute-start.14 = (bf16[256,1,2048]{2,0,1:T(8,128)(2,1)}, bf16[256,1,2048]{2,0,1:T(8,128)(2,1)S(1)}, u32[]{:S(2)}, u32[]{:S(2)}) collective-permute-start(bf16[256,1,2048]{2,0,1:T(8,128)(2,1)} %bitcast.102), channel_id=1, source_target_pairs={{60,0},{64,4},{68,8},{72,12},{76,16},{80,20},{84,24},{88,28},{92,3... | collective-permute-start | bytes 3145736 | tf_op jit(solution)/shard_map/ppermute | solution.py:13
  7.8 52.9 %collective-permute-start.13 = (bf16[256,1,2048]{2,0,1:T(8,128)(2,1)}, bf16[256,1,2048]{2,0,1:T(8,128)(2,1)S(1)}, u32[]{:S(2)}, u32[]{:S(2)}) collective-permute-start(bf16[256,1,2048]{2,0,1:T(8,128)(2,1)} %bitcast.103), channel_id=1, source_target_pairs={{56,0},{60,4},{64,8},{68,12},{72,16},{76,20},{80,24},{84,28},{88,3... | collective-permute-start | bytes 3145736 | tf_op jit(solution)/shard_map/ppermute | solution.py:13
  9.1 53.0 %collective-permute-start.12 = (bf16[256,1,2048]{2,0,1:T(8,128)(2,1)}, bf16[256,1,2048]{2,0,1:T(8,128)(2,1)S(1)}, u32[]{:S(2)}, u32[]{:S(2)}) collective-permute-start(bf16[256,1,2048]{2,0,1:T(8,128)(2,1)} %bitcast.104), channel_id=1, source_target_pairs={{52,0},{56,4},{60,8},{64,12},{68,16},{72,20},{76,24},{80,28},{84,3... | collective-permute-start | bytes 3145736 | tf_op jit(solution)/shard_map/ppermute | solution.py:13
  10.4 53.0 %collective-permute-start.11 = (bf16[256,1,2048]{2,0,1:T(8,128)(2,1)}, bf16[256,1,2048]{2,0,1:T(8,128)(2,1)S(1)}, u32[]{:S(2)}, u32[]{:S(2)}) collective-permute-start(bf16[256,1,2048]{2,0,1:T(8,128)(2,1)} %bitcast.105), channel_id=1, source_target_pairs={{48,0},{52,4},{56,8},{60,12},{64,16},{68,20},{72,24},{76,28},{80,3... | collective-permute-start | bytes 3145736 | tf_op jit(solution)/shard_map/ppermute | solution.py:13
  11.7 182.1 %collective-permute-start.10 = (bf16[256,1,2048]{2,0,1:T(8,128)(2,1)}, bf16[256,1,2048]{2,0,1:T(8,128)(2,1)S(1)}, u32[]{:S(2)}, u32[]{:S(2)}) collective-permute-start(bf16[256,1,2048]{2,0,1:T(8,128)(2,1)} %bitcast.106), channel_id=1, source_target_pairs={{44,0},{48,4},{52,8},{56,12},{60,16},{64,20},{68,24},{72,28},{76,3... | collective-permute-start | bytes 3145736 | tf_op jit(solution)/shard_map/ppermute | solution.py:13
  59.5 153.5 %collective-permute-start.9 = (bf16[256,1,2048]{2,0,1:T(8,128)(2,1)}, bf16[256,1,2048]{2,0,1:T(8,128)(2,1)S(1)}, u32[]{:S(2)}, u32[]{:S(2)}) collective-permute-start(bf16[256,1,2048]{2,0,1:T(8,128)(2,1)} %bitcast.107), channel_id=1, source_target_pairs={{40,0},{44,4},{48,8},{52,12},{56,16},{60,20},{64,24},{68,28},{72,3... | collective-permute-start | bytes 3145736 | tf_op jit(solution)/shard_map/ppermute | solution.py:13
  60.8 187.0 %collective-permute-start.8 = (bf16[256,1,2048]{2,0,1:T(8,128)(2,1)}, bf16[256,1,2048]{2,0,1:T(8,128)(2,1)S(1)}, u32[]{:S(2)}, u32[]{:S(2)}) collective-permute-start(bf16[256,1,2048]{2,0,1:T(8,128)(2,1)} %bitcast.108), channel_id=1, source_target_pairs={{36,0},{40,4},{44,8},{48,12},{52,16},{56,20},{60,24},{64,28},{68,3... | collective-permute-start | bytes 3145736 | tf_op jit(solution)/shard_map/ppermute | solution.py:13
  62.1 189.6 %copy-start.2 = (bf16[256,1,2048]{2,0,1:T(8,128)(2,1)}, bf16[256,1,2048]{2,0,1:T(8,128)(2,1)S(1)}, u32[]{:S(2)}) copy-start(bf16[256,1,2048]{2,0,1:T(8,128)(2,1)S(1)} %collective-permute-done.12) | copy-start | bytes 3145732
  62.1 187.0 %collective-permute-start.7 = (bf16[256,1,2048]{2,0,1:T(8,128)(2,1)}, bf16[256,1,2048]{2,0,1:T(8,128)(2,1)S(1)}, u32[]{:S(2)}, u32[]{:S(2)}) collective-permute-start(bf16[256,1,2048]{2,0,1:T(8,128)(2,1)} %bitcast.109), channel_id=1, source_target_pairs={{32,0},{36,4},{40,8},{44,12},{48,16},{52,20},{56,24},{60,28},{64,3... | collective-permute-start | bytes 3145736 | tf_op jit(solution)/shard_map/ppermute | solution.py:13
  63.4 188.3 %copy-start.3 = (bf16[256,1,2048]{2,0,1:T(8,128)(2,1)}, bf16[256,1,2048]{2,0,1:T(8,128)(2,1)S(1)}, u32[]{:S(2)}) copy-start(bf16[256,1,2048]{2,0,1:T(8,128)(2,1)S(1)} %collective-permute-done.11) | copy-start | bytes 3145732
  63.4 187.0 %collective-permute-start.6 = (bf16[256,1,2048]{2,0,1:T(8,128)(2,1)}, bf16[256,1,2048]{2,0,1:T(8,128)(2,1)S(1)}, u32[]{:S(2)}, u32[]{:S(2)}) collective-permute-start(bf16[256,1,2048]{2,0,1:T(8,128)(2,1)} %bitcast.110), channel_id=1, source_target_pairs={{28,0},{32,4},{36,8},{40,12},{44,16},{48,20},{52,24},{56,28},{60,3... | collective-permute-start | bytes 3145736 | tf_op jit(solution)/shard_map/ppermute | solution.py:13
  193.8 57.9 %copy-start.4 = (bf16[256,1,2048]{2,0,1:T(8,128)(2,1)}, bf16[256,1,2048]{2,0,1:T(8,128)(2,1)S(1)}, u32[]{:S(2)}) copy-start(bf16[256,1,2048]{2,0,1:T(8,128)(2,1)S(1)} %collective-permute-done.10) | copy-start | bytes 3145732
  193.8 57.9 %collective-permute-start.5 = (bf16[256,1,2048]{2,0,1:T(8,128)(2,1)}, bf16[256,1,2048]{2,0,1:T(8,128)(2,1)S(1)}, u32[]{:S(2)}, u32[]{:S(2)}) collective-permute-start(bf16[256,1,2048]{2,0,1:T(8,128)(2,1)} %bitcast.111), channel_id=1, source_target_pairs={{24,0},{28,4},{32,8},{36,12},{40,16},{44,20},{48,24},{52,28},{56,3... | collective-permute-start | bytes 3145736 | tf_op jit(solution)/shard_map/ppermute | solution.py:13
  213.0 38.8 %copy-start.5 = (bf16[256,1,2048]{2,0,1:T(8,128)(2,1)}, bf16[256,1,2048]{2,0,1:T(8,128)(2,1)S(1)}, u32[]{:S(2)}) copy-start(bf16[256,1,2048]{2,0,1:T(8,128)(2,1)S(1)} %collective-permute-done.9) | copy-start | bytes 3145732
  213.0 117.0 %collective-permute-start.4 = (bf16[256,1,2048]{2,0,1:T(8,128)(2,1)}, bf16[256,1,2048]{2,0,1:T(8,128)(2,1)}, u32[]{:S(2)}, u32[]{:S(2)}) collective-permute-start(bf16[256,1,2048]{2,0,1:T(8,128)(2,1)} %bitcast.112), channel_id=1, source_target_pairs={{20,0},{24,4},{28,8},{32,12},{36,16},{40,20},{44,24},{48,28},{52,3... | collective-permute-start | bytes 3145736 | tf_op jit(solution)/shard_map/ppermute | solution.py:13
  247.8 4.0 copy-start.6
  247.8 82.2 %collective-permute-start.3 = (bf16[256,1,2048]{2,0,1:T(8,128)(2,1)}, bf16[256,1,2048]{2,0,1:T(8,128)(2,1)}, u32[]{:S(2)}, u32[]{:S(2)}) collective-permute-start(bf16[256,1,2048]{2,0,1:T(8,128)(2,1)} %bitcast.113), channel_id=1, source_target_pairs={{16,0},{20,4},{24,8},{28,12},{32,16},{36,20},{40,24},{44,28},{48,3... | collective-permute-start | bytes 3145736 | tf_op jit(solution)/shard_map/ppermute | solution.py:13
  249.1 2.7 copy-start.7
  249.1 126.2 %collective-permute-start.2 = (bf16[256,1,2048]{2,0,1:T(8,128)(2,1)}, bf16[256,1,2048]{2,0,1:T(8,128)(2,1)}, u32[]{:S(2)}, u32[]{:S(2)}) collective-permute-start(bf16[256,1,2048]{2,0,1:T(8,128)(2,1)} %bitcast.114), channel_id=1, source_target_pairs={{12,0},{16,4},{20,8},{24,12},{28,16},{32,20},{36,24},{40,28},{44,3... | collective-permute-start | bytes 3145736 | tf_op jit(solution)/shard_map/ppermute | solution.py:13
  250.4 1.4 copy-start.8
  250.4 124.9 %collective-permute-start.1 = (bf16[256,1,2048]{2,0,1:T(8,128)(2,1)}, bf16[256,1,2048]{2,0,1:T(8,128)(2,1)}, u32[]{:S(2)}, u32[]{:S(2)}) collective-permute-start(bf16[256,1,2048]{2,0,1:T(8,128)(2,1)} %bitcast.115), channel_id=1, source_target_pairs={{8,0},{12,4},{16,8},{20,12},{24,16},{28,20},{32,24},{36,28},{40,32... | collective-permute-start | bytes 3145736 | tf_op jit(solution)/shard_map/ppermute | solution.py:13
  251.8 1.1 copy-start.9
  252.8 122.5 %collective-permute-start = (bf16[256,1,2048]{2,0,1:T(8,128)(2,1)}, bf16[256,1,2048]{2,0,1:T(8,128)(2,1)}, u32[]{:S(2)}, u32[]{:S(2)}) collective-permute-start(bf16[256,1,2048]{2,0,1:T(8,128)(2,1)} %bitcast.116), channel_id=1, source_target_pairs={{4,0},{8,4},{12,8},{16,12},{20,16},{24,20},{28,24},{32,28},{36,32}... | collective-permute-start | bytes 3145736 | tf_op jit(solution)/shard_map/ppermute | solution.py:13
  316.7 13.2 %copy-start = (f32[16,2048]{1,0:T(8,128)S(1)}, f32[16,2048]{1,0:T(8,128)}, u32[]{:S(2)}) copy-start(f32[16,2048]{1,0:T(8,128)} %param.4) | copy-start | bytes 393220
  316.7 58.6 %copy-start.1 = (bf16[256,2048]{1,0:T(8,128)(2,1)S(1)}, bf16[256,2048]{1,0:T(8,128)(2,1)}, u32[]{:S(2)}) copy-start(bf16[256,2048]{1,0:T(8,128)(2,1)} %param.3) | copy-start | bytes 3145732
  626.2 6.2 slice-start
  626.9 5.6 slice-start.1
Sparse Core Ops, SparseCore 0:
  637.0 146.1 reduce-scatter.1
where the time goes:
time: 794 us; the launch traced here: 792 us
  waiting for transfers between devices  419 us (53%)
  blocking collectives  198 us (25%)
  local copies, waits for them, and re-layouts  64.5 us (8%)
  other arithmetic  56.4 us (7%)
  matrix products  21.5 us (3%)
  starting transfers between devices  19.3 us (2%)
  between operations  13.8 us (2%)
    ppermute x15, waiting for transfers between devices, shifted(): lax.ppermute(value, axis, [(source, source + steps) for source in range(i...  272 us
    all_to_all x1, blocking collectives, local(): lax.all_to_all(spectra, 'tm', split_axis=1, concat_axis=0, tiled=True)  198 us
    reduce_scatter x1, waiting for transfers between devices, local(): lax.psum_scatter(form_beams(for_real, for_imag, beam_weights), 'feed', sc...  146 us
    another operation x1, other arithmetic  34.9 us
    another operation x1, local copies, waits for them, and re-layouts, dft_table(): jnp.stack([jnp.cos(angles) * norming, -jnp.sin(angles) * norming], axis=2)  21.5 us
    ppermute x15, starting transfers between devices, shifted(): lax.ppermute(value, axis, [(source, source + steps) for source in range(i...  19.3 us
  transfers between devices with their start and end apart: 16, of which 6 were waited for; matrix products, arithmetic and copies ran while one was open for 10% of the time, Pallas kernels for 0%

commit v1 on v0

--- a/solution.py
+++ b/solution.py
@@ -74,7 +74,10 @@
     spectra = jnp.einsum(
         "ftk,kc->tcf", filtered, transform, preferred_element_type=jnp.float32
     ).astype(jnp.bfloat16)
-    turned = lax.all_to_all(spectra, "tm", split_axis=1, concat_axis=0, tiled=True)
+    turned = jnp.concatenate(
+        lax.all_to_all(jnp.stack(jnp.split(spectra, lax.axis_size("tm"), axis=1)), "tm", 0, 0),
+        axis=0,
+    )
     total_frames, paired, feed_width = turned.shape
     per_group = paired // 2
     arranged = turned.reshape(total_frames, per_group, 2, feed_width)

time: 794 us -> 756 us (0.952)
  local copies, waits for them, and re-layouts: 64.5 us -> 37.8 us
  other arithmetic: 56.4 us -> 45.2 us
    convert_element_type x1 -> x0, local copies, waits for them, and re-layouts: 11.7 us -> none  [local(): spectra = jnp.einsum('ftk,kc->tcf', filtered, transform, preferred_elemen...]
    all_to_all x1 -> x0, local copies, waits for them, and re-layouts: 11 us -> none  [local(): lax.all_to_all(spectra, 'tm', split_axis=1, concat_axis=0, tiled=True)]
    unnamed x2 -> x1, other arithmetic: 10.8 us -> 0.01 us
where the time goes in v1:
time: 756 us; the launch traced here: 755 us
  waiting for transfers between devices  419 us (55%)
  blocking collectives  198 us (26%)
  other arithmetic  45.2 us (6%)
  local copies, waits for them, and re-layouts  37.8 us (5%)
  matrix products  21.3 us (3%)
  starting transfers between devices  19.3 us (3%)
  between operations  14.3 us (2%)
    ppermute x15, waiting for transfers between devices, shifted(): lax.ppermute(value, axis, [(source, source + steps) for source in range(i...  272 us
    all_to_all x1, blocking collectives, local(): lax.all_to_all(jnp.stack(jnp.split(spectra, lax.axis_size('tm'), axis=1))...  198 us
    reduce_scatter x1, waiting for transfers between devices, local(): lax.psum_scatter(form_beams(for_real, for_imag, beam_weights), 'feed', sc...  146 us
    another operation x1, other arithmetic  34.9 us
    another operation x1, local copies, waits for them, and re-layouts, dft_table(): jnp.stack([jnp.cos(angles) * norming, -jnp.sin(angles) * norming], axis=2)  21.5 us
    ppermute x15, starting transfers between devices, shifted(): lax.ppermute(value, axis, [(source, source + steps) for source in range(i...  19.3 us
  transfers between devices with their start and end apart: 16, of which 6 were waited for; matrix products, arithmetic and copies ran while one was open for 10% of the time, Pallas kernels for 0%

profile of v1, /device:TPU:1, one launch (start us, length us, event | category | flops | bytes accessed | tf_op | source)
XLA Modules:
  0.0 754.7 jit_solution(196316251312182905)
XLA Ops:
  6.5 1.3 collective-permute-start.14
  7.8 1.3 collective-permute-start.13
  9.1 1.3 collective-permute-start.12
  10.4 1.3 collective-permute-start.11
  11.7 1.3 collective-permute-start.10
  13.0 46.5 %collective-permute-done.14 = bf16[256,1,2048]{2,0,1:T(8,128)(2,1)S(1)} collective-permute-done((bf16[256,1,2048]{2,0,1:T(8,128)(2,1)}, bf16[256,1,2048]{2,0,1:T(8,128)(2,1)S(1)}, u32[]{:S(2)}, u32[]{:S(2)}) %collective-permute-start.14) | collective-permute-done | bytes 1048608 | tf_op jit(solution)/shard_map/ppermute | solution.py:13
  59.5 1.3 collective-permute-start.9
  60.8 0.0 collective-permute-done.13
  60.8 1.3 collective-permute-start.8
  62.1 0.0 collective-permute-done.12
  62.1 1.3 collective-permute-start.7
  63.4 0.0 collective-permute-done.11
  63.4 1.3 collective-permute-start.6
  64.7 129.1 %collective-permute-done.10 = bf16[256,1,2048]{2,0,1:T(8,128)(2,1)S(1)} collective-permute-done((bf16[256,1,2048]{2,0,1:T(8,128)(2,1)}, bf16[256,1,2048]{2,0,1:T(8,128)(2,1)S(1)}, u32[]{:S(2)}, u32[]{:S(2)}) %collective-permute-start.10) | collective-permute-done | bytes 1048608 | tf_op jit(solution)/shard_map/ppermute | solution.py:13
  193.8 1.3 collective-permute-start.5
  195.1 17.9 %collective-permute-done.9 = bf16[256,1,2048]{2,0,1:T(8,128)(2,1)S(1)} collective-permute-done((bf16[256,1,2048]{2,0,1:T(8,128)(2,1)}, bf16[256,1,2048]{2,0,1:T(8,128)(2,1)S(1)}, u32[]{:S(2)}, u32[]{:S(2)}) %collective-permute-start.9) | collective-permute-done | bytes 1048608 | tf_op jit(solution)/shard_map/ppermute | solution.py:13
  213.0 1.3 collective-permute-start.4
  214.2 33.5 %collective-permute-done.8 = bf16[256,1,2048]{2,0,1:T(8,128)(2,1)S(1)} collective-permute-done((bf16[256,1,2048]{2,0,1:T(8,128)(2,1)}, bf16[256,1,2048]{2,0,1:T(8,128)(2,1)S(1)}, u32[]{:S(2)}, u32[]{:S(2)}) %collective-permute-start.8) | collective-permute-done | bytes 1048608 | tf_op jit(solution)/shard_map/ppermute | solution.py:13
  247.8 1.3 collective-permute-start.3
  249.1 0.0 collective-permute-done.7
  249.1 1.3 collective-permute-start.2
  250.4 0.0 collective-permute-done.6
  250.4 1.3 collective-permute-start.1
  251.7 0.0 collective-permute-done.5
  251.8 1.1 copy-done.9
  252.9 1.3 collective-permute-start
  254.2 34.9 %multiply_convert_fusion = (bf16[2048,1024,1]{1,0,2:T(8,128)(2,1)S(1)}, bf16[2048,1024,1]{1,0,2:T(8,128)(2,1)}) fusion(), kind=kLoop, calls=%fused_computation.7 | loop fusion | flops 39845888 | bytes 8388608 | tf_op jit(solution)/shard_map/convert.1
  289.0 6.2 pad_maximum_fusion
  295.2 21.5 %copy.17 = bf16[2048,1024,2]{0,2,1:T(2,128)(2,1)} copy(bf16[2048,1024,2]{1,0,2:T(8,128)(2,1)} %pad_maximum_fusion) | data formatting | bytes 16777216 | tf_op jit(solution)/shard_map/stack | solution.py:22
  316.7 13.2 %convert_element_type.85 = bf16[2048,2048]{0,1:T(8,128)(2,1)} reshape(bf16[2048,1024,2]{0,2,1:T(2,128)(2,1)} %copy.17) | data formatting | bytes 16777216 | tf_op jit(solution)/shard_map/convert_element_type | solution.py:23
  330.0 0.1 fusion.57
  330.1 0.0 collective-permute-done.3
  330.1 45.2 %collective-permute-done.2 = bf16[256,1,2048]{2,0,1:T(8,128)(2,1)} collective-permute-done((bf16[256,1,2048]{2,0,1:T(8,128)(2,1)}, bf16[256,1,2048]{2,0,1:T(8,128)(2,1)}, u32[]{:S(2)}, u32[]{:S(2)}) %collective-permute-start.2) | collective-permute-done | bytes 1048608 | tf_op jit(solution)/shard_map/ppermute | solution.py:13
  375.3 14.0 %fusion.10 = bf16[1,2048,256]{2,1,0:T(8,128)(2,1)S(1)} fusion(bf16[2048,2048]{0,1:T(8,128)(2,1)} %convert_element_type.85, bf16[256,1,2048]{2,0,1:T(8,128)(2,1)S(1)} %collective-permute-done.14, bf16[256,1,2048]{2,0,1:T(8,128)(2,1)S(1)} %collective-permute-done.13, bf16[256,1,2048]{2,0,1:T(8,128)(2,1)} %copy-done.2, bf16[256,1,2048]{2,0,1:T(8,128)(2,1)} %copy-done.3, ...), kind=kOutput, calls=%fused_computation.18 | convolution fusion | flops 2173173760 | bytes 26345472 | tf_op jit(solution)/shard_map/ftk,kc->tcf/dot_general | solution.py:74
  390.0 198.4 %all_to_all.5 = bf16[64,1,32,256]{3,2,1,0:T(8,128)(2,1)S(1)} all-to-all(bf16[64,1,32,256]{3,2,1,0:T(8,128)(2,1)S(1)} %constant_dynamic-update-slice_fusion), channel_id=1, replica_groups=mesh['tm'=64,'feed'=4] {'tm'}, dimensions={0} | all-to-all | bytes 2097152 | tf_op jit(solution)/shard_map/all_to_all | solution.py:78
  588.5 0.6 copy.25
  589.1 0.0 slice-start
  589.1 0.1 slice_negate_fusion
  589.2 0.0 slice-start.1
  589.2 5.4 fusion.29
  594.6 0.4 slice-done.1
  594.9 2.0 fusion.26
  596.9 2.5 pad_maximum_fusion.1
  599.4 0.0 reduce-scatter.2.cloned.1.call-update
  599.4 146.3 %reduce-scatter.2.cloned.1.call-done = f32[128,2,16,64]{0,3,2,1:T(8,128)} async-done(((f32[512,2,16,64]{0,3,2,1:T(8,128)}), f32[128,2,16,64]{0,3,2,1:T(8,128)}) %reduce-scatter.2.cloned.1.call-update) | async-done | bytes 1048592 | tf_op jit(solution)/shard_map/reduce_scatter | solution.py:85
  745.7 1.4 multiply_reduce_fusion
  747.1 0.1 bitcast_reduce_fusion
  747.2 0.6 copy.22
  (90 shorter events, 0.3 us)
Async XLA Ops:
  6.5 739.2 %reduce-scatter.2.cloned.1.call-start = ((), (), s32[]{:S(2)}) async-start(), calls=%async_computation.2 | async-start | bytes 5242880 | tf_op jit(solution)/shard_map/reduce_scatter | solution.py:85
  6.5 52.9 %collective-permute-start.14 = (bf16[256,1,2048]{2,0,1:T(8,128)(2,1)}, bf16[256,1,2048]{2,0,1:T(8,128)(2,1)S(1)}, u32[]{:S(2)}, u32[]{:S(2)}) collective-permute-start(bf16[256,1,2048]{2,0,1:T(8,128)(2,1)} %bitcast.354), channel_id=1, source_target_pairs={{60,0},{64,4},{68,8},{72,12},{76,16},{80,20},{84,24},{88,28},{92,3... | collective-permute-start | bytes 3145736 | tf_op jit(solution)/shard_map/ppermute | solution.py:13
  7.8 52.9 %collective-permute-start.13 = (bf16[256,1,2048]{2,0,1:T(8,128)(2,1)}, bf16[256,1,2048]{2,0,1:T(8,128)(2,1)S(1)}, u32[]{:S(2)}, u32[]{:S(2)}) collective-permute-start(bf16[256,1,2048]{2,0,1:T(8,128)(2,1)} %bitcast.355), channel_id=1, source_target_pairs={{56,0},{60,4},{64,8},{68,12},{72,16},{76,20},{80,24},{84,28},{88,3... | collective-permute-start | bytes 3145736 | tf_op jit(solution)/shard_map/ppermute | solution.py:13
  9.1 53.0 %collective-permute-start.12 = (bf16[256,1,2048]{2,0,1:T(8,128)(2,1)}, bf16[256,1,2048]{2,0,1:T(8,128)(2,1)S(1)}, u32[]{:S(2)}, u32[]{:S(2)}) collective-permute-start(bf16[256,1,2048]{2,0,1:T(8,128)(2,1)} %bitcast.356), channel_id=1, source_target_pairs={{52,0},{56,4},{60,8},{64,12},{68,16},{72,20},{76,24},{80,28},{84,3... | collective-permute-start | bytes 3145736 | tf_op jit(solution)/shard_map/ppermute | solution.py:13
  10.4 53.0 %collective-permute-start.11 = (bf16[256,1,2048]{2,0,1:T(8,128)(2,1)}, bf16[256,1,2048]{2,0,1:T(8,128)(2,1)S(1)}, u32[]{:S(2)}, u32[]{:S(2)}) collective-permute-start(bf16[256,1,2048]{2,0,1:T(8,128)(2,1)} %bitcast.357), channel_id=1, source_target_pairs={{48,0},{52,4},{56,8},{60,12},{64,16},{68,20},{72,24},{76,28},{80,3... | collective-permute-start | bytes 3145736 | tf_op jit(solution)/shard_map/ppermute | solution.py:13
  11.7 182.1 %collective-permute-start.10 = (bf16[256,1,2048]{2,0,1:T(8,128)(2,1)}, bf16[256,1,2048]{2,0,1:T(8,128)(2,1)S(1)}, u32[]{:S(2)}, u32[]{:S(2)}) collective-permute-start(bf16[256,1,2048]{2,0,1:T(8,128)(2,1)} %bitcast.358), channel_id=1, source_target_pairs={{44,0},{48,4},{52,8},{56,12},{60,16},{64,20},{68,24},{72,28},{76,3... | collective-permute-start | bytes 3145736 | tf_op jit(solution)/shard_map/ppermute | solution.py:13
  59.5 153.5 %collective-permute-start.9 = (bf16[256,1,2048]{2,0,1:T(8,128)(2,1)}, bf16[256,1,2048]{2,0,1:T(8,128)(2,1)S(1)}, u32[]{:S(2)}, u32[]{:S(2)}) collective-permute-start(bf16[256,1,2048]{2,0,1:T(8,128)(2,1)} %bitcast.359), channel_id=1, source_target_pairs={{40,0},{44,4},{48,8},{52,12},{56,16},{60,20},{64,24},{68,28},{72,3... | collective-permute-start | bytes 3145736 | tf_op jit(solution)/shard_map/ppermute | solution.py:13
  60.8 187.0 %collective-permute-start.8 = (bf16[256,1,2048]{2,0,1:T(8,128)(2,1)}, bf16[256,1,2048]{2,0,1:T(8,128)(2,1)S(1)}, u32[]{:S(2)}, u32[]{:S(2)}) collective-permute-start(bf16[256,1,2048]{2,0,1:T(8,128)(2,1)} %bitcast.360), channel_id=1, source_target_pairs={{36,0},{40,4},{44,8},{48,12},{52,16},{56,20},{60,24},{64,28},{68,3... | collective-permute-start | bytes 3145736 | tf_op jit(solution)/shard_map/ppermute | solution.py:13
  62.1 189.6 %copy-start.2 = (bf16[256,1,2048]{2,0,1:T(8,128)(2,1)}, bf16[256,1,2048]{2,0,1:T(8,128)(2,1)S(1)}, u32[]{:S(2)}) copy-start(bf16[256,1,2048]{2,0,1:T(8,128)(2,1)S(1)} %collective-permute-done.12) | copy-start | bytes 3145732
  62.1 187.0 %collective-permute-start.7 = (bf16[256,1,2048]{2,0,1:T(8,128)(2,1)}, bf16[256,1,2048]{2,0,1:T(8,128)(2,1)S(1)}, u32[]{:S(2)}, u32[]{:S(2)}) collective-permute-start(bf16[256,1,2048]{2,0,1:T(8,128)(2,1)} %bitcast.361), channel_id=1, source_target_pairs={{32,0},{36,4},{40,8},{44,12},{48,16},{52,20},{56,24},{60,28},{64,3... | collective-permute-start | bytes 3145736 | tf_op jit(solution)/shard_map/ppermute | solution.py:13
  63.4 188.3 %copy-start.3 = (bf16[256,1,2048]{2,0,1:T(8,128)(2,1)}, bf16[256,1,2048]{2,0,1:T(8,128)(2,1)S(1)}, u32[]{:S(2)}) copy-start(bf16[256,1,2048]{2,0,1:T(8,128)(2,1)S(1)} %collective-permute-done.11) | copy-start | bytes 3145732
  63.4 187.0 %collective-permute-start.6 = (bf16[256,1,2048]{2,0,1:T(8,128)(2,1)}, bf16[256,1,2048]{2,0,1:T(8,128)(2,1)S(1)}, u32[]{:S(2)}, u32[]{:S(2)}) collective-permute-start(bf16[256,1,2048]{2,0,1:T(8,128)(2,1)} %bitcast.362), channel_id=1, source_target_pairs={{28,0},{32,4},{36,8},{40,12},{44,16},{48,20},{52,24},{56,28},{60,3... | collective-permute-start | bytes 3145736 | tf_op jit(solution)/shard_map/ppermute | solution.py:13
  193.8 57.9 %copy-start.4 = (bf16[256,1,2048]{2,0,1:T(8,128)(2,1)}, bf16[256,1,2048]{2,0,1:T(8,128)(2,1)S(1)}, u32[]{:S(2)}) copy-start(bf16[256,1,2048]{2,0,1:T(8,128)(2,1)S(1)} %collective-permute-done.10) | copy-start | bytes 3145732
  193.8 57.9 %collective-permute-start.5 = (bf16[256,1,2048]{2,0,1:T(8,128)(2,1)}, bf16[256,1,2048]{2,0,1:T(8,128)(2,1)S(1)}, u32[]{:S(2)}, u32[]{:S(2)}) collective-permute-start(bf16[256,1,2048]{2,0,1:T(8,128)(2,1)} %bitcast.363), channel_id=1, source_target_pairs={{24,0},{28,4},{32,8},{36,12},{40,16},{44,20},{48,24},{52,28},{56,3... | collective-permute-start | bytes 3145736 | tf_op jit(solution)/shard_map/ppermute | solution.py:13
  213.0 38.8 %copy-start.5 = (bf16[256,1,2048]{2,0,1:T(8,128)(2,1)}, bf16[256,1,2048]{2,0,1:T(8,128)(2,1)S(1)}, u32[]{:S(2)}) copy-start(bf16[256,1,2048]{2,0,1:T(8,128)(2,1)S(1)} %collective-permute-done.9) | copy-start | bytes 3145732
  213.0 117.1 %collective-permute-start.4 = (bf16[256,1,2048]{2,0,1:T(8,128)(2,1)}, bf16[256,1,2048]{2,0,1:T(8,128)(2,1)}, u32[]{:S(2)}, u32[]{:S(2)}) collective-permute-start(bf16[256,1,2048]{2,0,1:T(8,128)(2,1)} %bitcast.364), channel_id=1, source_target_pairs={{20,0},{24,4},{28,8},{32,12},{36,16},{40,20},{44,24},{48,28},{52,3... | collective-permute-start | bytes 3145736 | tf_op jit(solution)/shard_map/ppermute | solution.py:13
  247.8 4.0 copy-start.6
  247.8 82.3 %collective-permute-start.3 = (bf16[256,1,2048]{2,0,1:T(8,128)(2,1)}, bf16[256,1,2048]{2,0,1:T(8,128)(2,1)}, u32[]{:S(2)}, u32[]{:S(2)}) collective-permute-start(bf16[256,1,2048]{2,0,1:T(8,128)(2,1)} %bitcast.365), channel_id=1, source_target_pairs={{16,0},{20,4},{24,8},{28,12},{32,16},{36,20},{40,24},{44,28},{48,3... | collective-permute-start | bytes 3145736 | tf_op jit(solution)/shard_map/ppermute | solution.py:13
  249.1 2.7 copy-start.7
  249.1 126.2 %collective-permute-start.2 = (bf16[256,1,2048]{2,0,1:T(8,128)(2,1)}, bf16[256,1,2048]{2,0,1:T(8,128)(2,1)}, u32[]{:S(2)}, u32[]{:S(2)}) collective-permute-start(bf16[256,1,2048]{2,0,1:T(8,128)(2,1)} %bitcast.366), channel_id=1, source_target_pairs={{12,0},{16,4},{20,8},{24,12},{28,16},{32,20},{36,24},{40,28},{44,3... | collective-permute-start | bytes 3145736 | tf_op jit(solution)/shard_map/ppermute | solution.py:13
  250.4 1.4 copy-start.8
  250.4 124.9 %collective-permute-start.1 = (bf16[256,1,2048]{2,0,1:T(8,128)(2,1)}, bf16[256,1,2048]{2,0,1:T(8,128)(2,1)}, u32[]{:S(2)}, u32[]{:S(2)}) collective-permute-start(bf16[256,1,2048]{2,0,1:T(8,128)(2,1)} %bitcast.367), channel_id=1, source_target_pairs={{8,0},{12,4},{16,8},{20,12},{24,16},{28,20},{32,24},{36,28},{40,32... | collective-permute-start | bytes 3145736 | tf_op jit(solution)/shard_map/ppermute | solution.py:13
  251.8 1.1 copy-start.9
  252.9 122.5 %collective-permute-start = (bf16[256,1,2048]{2,0,1:T(8,128)(2,1)}, bf16[256,1,2048]{2,0,1:T(8,128)(2,1)}, u32[]{:S(2)}, u32[]{:S(2)}) collective-permute-start(bf16[256,1,2048]{2,0,1:T(8,128)(2,1)} %bitcast.368), channel_id=1, source_target_pairs={{4,0},{8,4},{12,8},{16,12},{20,16},{24,20},{28,24},{32,28},{36,32}... | collective-permute-start | bytes 3145736 | tf_op jit(solution)/shard_map/ppermute | solution.py:13
  316.7 13.2 %copy-start = (f32[16,2048]{1,0:T(8,128)S(1)}, f32[16,2048]{1,0:T(8,128)}, u32[]{:S(2)}) copy-start(f32[16,2048]{1,0:T(8,128)} %param.4) | copy-start | bytes 393220
  316.7 58.6 %copy-start.1 = (bf16[256,2048]{1,0:T(8,128)(2,1)S(1)}, bf16[256,2048]{1,0:T(8,128)(2,1)}, u32[]{:S(2)}) copy-start(bf16[256,2048]{1,0:T(8,128)(2,1)} %param.3) | copy-start | bytes 3145732
  589.1 5.5 slice-start
  589.2 5.8 slice-start.1
Sparse Core Ops, SparseCore 0:
  599.5 146.1 reduce-scatter.1
